TPU v7x, 32 devices: a whole 2x2x4 slice. The times are simulated.
32 devices in a mesh: year: 8 (over z, x), region: 4 (over y, core).
Axes of the slice: x: 2, y: 2, z: 4, core: 2. Of those that a mesh axis runs over, the one named last changes fastest.
Arguments:
- daily_temps: bfloat16 [8, 22, 512], P('year', None, 'region'), may hold values from -6 to 6
- land_mask: int32 [512], P('region'), may hold values 0 or 1
Outputs:
- coarse_threshold: float32 [8, 512], P('year', 'region')
- refined_threshold: float32 [8, 512], P('year', 'region')
All inputs are finite; a program needn't handle non-finite values. No bound on the sum of `land_mask` on one device may be relied on, other than what follows from the above.
Results may differ from a plain program's by a relative error of at most 0.0013.
Values may be sent and summed in bfloat16 or wider, within the bound.
No kernel may reach another device: no remote copies, remote signals or barrier semaphores. Data moves between devices by JAX's collectives and lax.ppermute only.
A program may use at most 64 MiB of HBM per device.

v0:
```python
import jax
import jax.numpy as jnp
from jax import lax
from jax.sharding import PartitionSpec as P

WIN = 15
BINS = 256
VALUE_RANGE = 12.8
QUANT_LEVEL = 0.9
SHARPNESS = 32.0
KERNEL_SCALE = 0.25
STEP_SIZE = 2.0


def extended_2(array, sides, width):
    for axis, dim in sides:
        devices, length = (lax.axis_size(axis), array.shape[dim])
        up = [(i, (i + 1) % devices) for i in range(devices)]
        down = [(j, i) for i, j in up]
        last = lax.slice_in_dim(array, length - width, length, axis=dim)
        leading = lax.slice_in_dim(array, 0, width, axis=dim)
        before = lax.ppermute(last, axis, up)
        after = lax.ppermute(leading, axis, down)
        array = jnp.concatenate([before, array, after], axis=dim)
    return array


def smooth_field(extended, flags):
    center = extended[..., 1:-1]
    same_west = 1.0 - jnp.abs(flags[1:-1] - flags[:-2])
    same_east = 1.0 - jnp.abs(flags[1:-1] - flags[2:])
    mixed = center + same_west * extended[..., :-2] + same_east * extended[..., 2:]
    return (mixed / (1.0 + same_west + same_east)).astype(jnp.bfloat16)


def bin_weights(year_field, bin_count):
    width = VALUE_RANGE / bin_count
    scaled = jnp.clip(
        (year_field.astype(jnp.float32) + 0.5 * VALUE_RANGE) / width, 0.0, bin_count - 1.0
    )
    centers = jnp.arange(bin_count, dtype=jnp.float32)
    return jnp.maximum(0.0, 1.0 - jnp.abs(scaled[..., None] - centers)).astype(jnp.bfloat16)


def quantile(histogram, count_all, bin_count):
    width = VALUE_RANGE / bin_count
    cumulative = jnp.cumsum(histogram, axis=-1)
    ranks = jnp.clip(0.5 + SHARPNESS * (QUANT_LEVEL - cumulative / count_all), 0.0, 1.0)
    return -0.5 * VALUE_RANGE + width * jnp.sum(ranks, axis=-1)


def day_band(row_count, days_in):
    row_day = lax.broadcasted_iota(jnp.int32, (row_count, days_in), 0)
    column_day = lax.broadcasted_iota(jnp.int32, (row_count, days_in), 1)
    inside = (column_day >= row_day) & (column_day < row_day + WIN)
    return jnp.where(inside, 1.0, 0.0).astype(jnp.bfloat16)


def window_cdf(threshold, year_field):
    cal_days = threshold.shape[0]
    samples = year_field.astype(jnp.float32)
    running = jnp.zeros(threshold.shape, jnp.float32)
    for offset in range(WIN):
        window = samples[:, offset : offset + cal_days, :]
        running = running + jnp.sum(
            jax.nn.sigmoid((threshold[None] - window) / KERNEL_SCALE), axis=0
        )
    return running


def shards(daily_temps, land_mask):
    days_in = daily_temps.shape[1]
    lon_cells = daily_temps.shape[2]
    year_count = lax.axis_size("year")
    cal_days = days_in - WIN + 1
    cal_own = cal_days // year_count
    count_all = float(year_count * WIN)
    flag_row = land_mask.astype(jnp.bfloat16)[None, :]
    stacked = jnp.concatenate([daily_temps[0], flag_row], axis=0)
    extended = extended_2(stacked, (("region", 1),), 1)
    smoothed = smooth_field(
        extended[:days_in].astype(jnp.float32), extended[days_in].astype(jnp.float32)
    )
    weights = bin_weights(smoothed, BINS).reshape(days_in, lon_cells * BINS)
    own_rows = lax.psum_scatter(
        jnp.dot(
            day_band(cal_own * lax.axis_size("year"), days_in),
            weights,
            preferred_element_type=jnp.float32,
        ),
        "year",
        scatter_dimension=0,
        tiled=True,
    )
    coarse = quantile(own_rows.reshape(cal_own, lon_cells, BINS), count_all, BINS)
    coarse_all = lax.all_gather(coarse, "year", axis=0, tiled=True)
    partial_cdf = window_cdf(coarse_all, smoothed[None])
    cdf_whole = lax.psum(partial_cdf, "year")
    own_cdf = lax.dynamic_slice_in_dim(cdf_whole, lax.axis_index("year") * cal_own, cal_own, 0)
    refined = coarse - STEP_SIZE * (own_cdf / count_all - QUANT_LEVEL)
    return (coarse, refined)


def solution(mesh):
    return jax.shard_map(
        shards,
        mesh=mesh,
        in_specs=(P("year", None, "region"), P("region")),
        out_specs=(P("year", "region"), P("year", "region")),
        check_vma=False,
    )
```

profile of v0, /device:TPU:0, one launch (start us, length us, event | category | flops | bytes accessed | tf_op | source)
XLA Modules:
  0.0 145.1 jit_solution(3068982300265254493)
XLA Ops:
  7.2 0.7 convert_bitcast_fusion.1
  7.9 0.8 slice_maximum_fusion
  8.7 2.4 %collective-permute-start.1 = (bf16[23,1]{1,0:T(8,128)(2,1)S(1)}, bf16[23,1]{1,0:T(8,128)(2,1)S(1)}, u32[]{:S(2)}, u32[]{:S(2)}) collective-permute-start(bf16[23,1]{1,0:T(8,128)(2,1)S(1)} %get-tuple-element.9), channel_id=1, source_target_pairs={{1,0},{2,1},{3,2},{0,3},{5,4},{6,5},{7,6},{4,7},{9,8},{10,9},{11,1... | collective-permute-start | bytes 146 | tf_op jit(solution)/shard_map/ppermute | solution.py:23
  11.2 0.1 copy.8
  11.2 1.2 collective-permute-done.1
  12.5 1.7 %collective-permute-done = bf16[23,1]{1,0:T(8,128)(2,1)S(1)} collective-permute-done((bf16[23,1]{1,0:T(8,128)(2,1)S(1)}, bf16[23,1]{1,0:T(8,128)(2,1)S(1)}, u32[]{:S(2)}, u32[]{:S(2)}) %collective-permute-start) | collective-permute-done | bytes 78 | tf_op jit(solution)/shard_map/ppermute | solution.py:22
  14.2 0.8 maximum_convert_fusion.2
  14.9 0.1 bitcast_add_fusion
  15.0 0.1 subtract_bitcast_fusion.1
  15.1 0.8 pad_maximum_fusion
  15.9 0.1 convert_bitcast_fusion
  16.0 0.4 sub.122
  16.4 0.3 pad.12
  16.8 1.8 %copy.7 = f32[3,8,128,256]{3,1,2,0:T(8,128)S(1)} copy(f32[3,8,128,256]{3,2,1,0:T(8,128)S(1)} %bitcast.36) | data formatting | bytes 6291456
  18.6 1.8 %fusion = f32[8,32768]{1,0:T(8,128)} fusion(f32[22,32768]{1,0:T(8,128)S(1)} %bitcast.35, f32[32768]{0:T(1024)S(1)} %bitcast.37, s32[8]{0:T(128)S(1)} %iota_add_fusion), kind=kOutput, calls=%fused_computation.1 | convolution fusion | flops 15139696 | bytes 4063264 | tf_op jit(solution)/shard_map/dot_general | solution.py:86
  20.5 0.6 dynamic-slice
  21.1 77.9 %all-reduce.3.cloned.1.call-done = f32[8,32768]{1,0:T(8,128)} async-done(((f32[8,32768]{1,0:T(8,128)}), f32[8,32768]{1,0:T(8,128)}) %all-reduce.3.cloned.1.call-update) | async-done | bytes 1048592
  99.0 2.0 %constant_dynamic-slice_fusion = f32[1,32768]{1,0:T(1,128)S(1)} fusion(f32[8,32768]{1,0:T(8,128)} %all-reduce.3.cloned.1.call-done, u32[]{:T(128)} %bitcast.13), kind=kLoop, calls=%fused_computation.140 | loop fusion | bytes 262148
  101.0 0.1 copy.6
  101.1 0.1 fusion.112
  101.3 0.2 clamp_reduce_fusion
  101.4 19.1 %all-gather.1 = f32[8,1,128]{2,1,0:T(1,128)S(1)} all-gather(f32[1,1,128]{2,1,0:T(1,128)S(1)} %fusion.106), channel_id=2, replica_groups=mesh['year'=8,'region'=4] {'year'}, dimensions={0}, use_global_device_ids=true | all-gather | bytes 4608 | tf_op jit(solution)/shard_map/all_gather | solution.py:96
  120.5 17.1 %psum.7 = f32[8,128]{1,0:T(8,128)S(1)} all-reduce(f32[8,128]{1,0:T(8,128)S(1)} %fusion.16), channel_id=1, replica_groups=mesh['year'=8,'region'=4] {'year'}, use_global_device_ids=true, to_apply=%region_4.5 | all-reduce | flops 1024 | bytes 8192 | tf_op jit(solution)/shard_map/psum | solution.py:98
  137.7 0.5 multiply_subtract_fusion
  (14 shorter events, 0.2 us)
Async XLA Ops:
  7.2 91.8 %all-reduce.3.cloned.1.call-start = ((), (), s32[]{:S(2)}) async-start(), calls=%async_computation | async-start | bytes 2097152
  8.7 3.8 %collective-permute-start.1 = (bf16[23,1]{1,0:T(8,128)(2,1)S(1)}, bf16[23,1]{1,0:T(8,128)(2,1)S(1)}, u32[]{:S(2)}, u32[]{:S(2)}) collective-permute-start(bf16[23,1]{1,0:T(8,128)(2,1)S(1)} %get-tuple-element.9), channel_id=1, source_target_pairs={{1,0},{2,1},{3,2},{0,3},{5,4},{6,5},{7,6},{4,7},{9,8},{10,9},{11,1... | collective-permute-start | bytes 146 | tf_op jit(solution)/shard_map/ppermute | solution.py:23
  11.1 3.1 %collective-permute-start = (bf16[23,1]{1,0:T(8,128)(2,1)S(1)}, bf16[23,1]{1,0:T(8,128)(2,1)S(1)}, u32[]{:S(2)}, u32[]{:S(2)}) collective-permute-start(bf16[23,1]{1,0:T(8,128)(2,1)S(1)} %get-tuple-element.8), channel_id=1, source_target_pairs={{0,1},{1,2},{2,3},{3,0},{4,5},{5,6},{6,7},{7,4},{8,9},{9,10},{10,1... | collective-permute-start | bytes 146 | tf_op jit(solution)/shard_map/ppermute | solution.py:22
  18.6 1.9 %copy-start = (u32[32]{0:T(128)S(1)}, u32[32]{0:T(128)}, u32[]{:S(2)}) copy-start(u32[32]{0:T(128)} %constant.71) | copy-start | bytes 388
Sparse Core Ops, SparseCore 0:
  20.6 78.3 all-reduce.2
where the time goes:
time: 145 us
  waiting for transfers between devices  80.9 us (56%)
  blocking collectives  36.2 us (25%)
  between operations  14.1 us (10%)
  local copies, waits for them, and re-layouts  5.36 us (4%)
  other arithmetic  4.19 us (3%)
  starting transfers between devices  2.45 us (2%)
  matrix products  1.83 us (1%)
    unnamed x2, waiting for transfers between devices  78 us
    all_gather x1, blocking collectives, shards(): coarse_all = lax.all_gather(coarse, 'year', axis=0, tiled=True)  19.1 us
    psum x1, blocking collectives, shards(): cdf_whole = lax.psum(partial_cdf, 'year')  17.1 us
    unnamed x8, local copies, waits for them, and re-layouts  4.8 us
  transfers between devices with their start and end apart: 3, of which 3 were waited for; matrix products, arithmetic and copies ran while one was open for 0% of the time, Pallas kernels for 0%

commit v1 on v0

--- a/solution.py
+++ b/solution.py
@@ -93,7 +93,12 @@
         tiled=True,
     )
     coarse = quantile(own_rows.reshape(cal_own, lon_cells, BINS), count_all, BINS)
-    coarse_all = lax.all_gather(coarse, "year", axis=0, tiled=True)
+    ring = [coarse]
+    for hop in range(7):
+        ring.append(lax.ppermute(ring[-1], "year", [(dev, (dev + 1) % 8) for dev in range(8)]))
+    coarse_all = jnp.roll(
+        jnp.concatenate(ring[::-1], axis=0), (lax.axis_index("year") + 1) * ring[0].shape[0], axis=0
+    )
     partial_cdf = window_cdf(coarse_all, smoothed[None])
     cdf_whole = lax.psum(partial_cdf, "year")
     own_cdf = lax.dynamic_slice_in_dim(cdf_whole, lax.axis_index("year") * cal_own, cal_own, 0)

time: 145 us -> 170 us (1.17)
  waiting for transfers between devices: 80.9 us -> 124 us
  blocking collectives: 36.2 us -> 17.1 us
    ppermute x0 -> x7, waiting for transfers between devices: none -> 42.4 us  [shards(): lax.ppermute(ring[-1], 'year', [(dev, (dev + 1) % 8) for dev in range(8)])]
    all_gather x1 -> x0, blocking collectives: 19.1 us -> none  [shards(): coarse_all = lax.all_gather(coarse, 'year', axis=0, tiled=True)]
    unnamed x2, waiting for transfers between devices: 78 us -> 80 us
    unnamed x8 -> x10, local copies, waits for them, and re-layouts: 4.8 us -> 4.8 us
  transfers between devices with their start and end apart: 3 -> 10, of which waited for: 3 -> 10; matrix products, arithmetic and copies ran while one was open for 0% -> 0% of each run, Pallas kernels for 0% -> 0%
where the time goes in v1:
time: 170 us
  waiting for transfers between devices  124 us (73%)
  blocking collectives  17.1 us (10%)
  between operations  14.1 us (8%)
  local copies, waits for them, and re-layouts  5.41 us (3%)
  other arithmetic  4.19 us (2%)
  starting transfers between devices  3.82 us (2%)
  matrix products  1.82 us (1%)
    unnamed x2, waiting for transfers between devices  80 us
    ppermute x7, waiting for transfers between devices, shards(): lax.ppermute(ring[-1], 'year', [(dev, (dev + 1) % 8) for dev in range(8)])  42.4 us
    psum x1, blocking collectives, shards(): cdf_whole = lax.psum(partial_cdf, 'year')  17.1 us
    unnamed x10, local copies, waits for them, and re-layouts  4.8 us
  transfers between devices with their start and end apart: 10, of which 10 were waited for; matrix products, arithmetic and copies ran while one was open for 0% of the time, Pallas kernels for 0%

profile of v1, /device:TPU:0, one launch (start us, length us, event | category | flops | bytes accessed | tf_op | source)
XLA Modules:
  0.0 170.1 jit_solution(14202258594101671444)
XLA Ops:
  7.2 0.7 convert_bitcast_fusion.1
  7.9 0.8 slice_maximum_fusion
  8.7 0.5 collective-permute-start
  9.2 2.0 %collective-permute-start.1 = (bf16[23,1]{1,0:T(8,128)(2,1)S(1)}, bf16[23,1]{1,0:T(8,128)(2,1)S(1)}, u32[]{:S(2)}, u32[]{:S(2)}) collective-permute-start(bf16[23,1]{1,0:T(8,128)(2,1)S(1)} %get-tuple-element.7), channel_id=1, source_target_pairs={{1,0},{2,1},{3,2},{0,3},{5,4},{6,5},{7,6},{4,7},{9,8},{10,9},{11,1... | collective-permute-start | bytes 146 | tf_op jit(solution)/shard_map/ppermute | solution.py:23
  11.3 1.2 collective-permute-done
  12.5 0.8 maximum_convert_fusion.2
  13.4 0.8 pad_maximum_fusion
  14.3 0.4 sub.126
  14.8 0.3 pad.12
  15.1 1.8 %copy.6 = f32[3,8,128,256]{3,1,2,0:T(8,128)S(1)} copy(f32[3,8,128,256]{3,2,1,0:T(8,128)S(1)} %bitcast.34) | data formatting | bytes 6291456
  16.9 1.8 %fusion = f32[8,32768]{1,0:T(8,128)} fusion(f32[22,32768]{1,0:T(8,128)S(1)} %bitcast.33, f32[32768]{0:T(1024)S(1)} %bitcast.35, s32[8]{0:T(128)S(1)} %iota_add_fusion), kind=kOutput, calls=%fused_computation.1 | convolution fusion | flops 15139696 | bytes 4063264 | tf_op jit(solution)/shard_map/dot_general | solution.py:86
  18.8 0.6 dynamic-slice
  19.4 79.9 %all-reduce.3.cloned.1.call-done = f32[8,32768]{1,0:T(8,128)} async-done(((f32[8,32768]{1,0:T(8,128)}), f32[8,32768]{1,0:T(8,128)}) %all-reduce.3.cloned.1.call-update) | async-done | bytes 1048592
  99.3 2.0 %constant_dynamic-slice_fusion = f32[1,32768]{1,0:T(1,128)S(1)} fusion(f32[8,32768]{1,0:T(8,128)} %all-reduce.3.cloned.1.call-done, u32[]{:T(128)} %bitcast.12), kind=kLoop, calls=%fused_computation.140 | loop fusion | bytes 262148
  101.8 1.3 collective-permute-start.2
  103.1 5.0 %collective-permute-done.2 = f32[1,128]{1,0:T(1,128)S(1)} collective-permute-done((f32[1,128]{1,0:T(1,128)S(1)}, f32[1,128]{1,0:T(1,128)S(1)}, u32[]{:S(2)}, u32[]{:S(2)}) %collective-permute-start.2) | collective-permute-done | bytes 544 | tf_op jit(solution)/shard_map/ppermute | solution.py:98
  108.1 6.2 %collective-permute-done.3 = f32[1,128]{1,0:T(1,128)S(1)} collective-permute-done((f32[1,128]{1,0:T(1,128)S(1)}, f32[1,128]{1,0:T(1,128)S(1)}, u32[]{:S(2)}, u32[]{:S(2)}) %collective-permute-start.3) | collective-permute-done | bytes 544 | tf_op jit(solution)/shard_map/ppermute | solution.py:98
  114.3 6.2 %collective-permute-done.4 = f32[1,128]{1,0:T(1,128)S(1)} collective-permute-done((f32[1,128]{1,0:T(1,128)S(1)}, f32[1,128]{1,0:T(1,128)S(1)}, u32[]{:S(2)}, u32[]{:S(2)}) %collective-permute-start.4) | collective-permute-done | bytes 544 | tf_op jit(solution)/shard_map/ppermute | solution.py:98
  120.6 6.2 %collective-permute-done.5 = f32[1,128]{1,0:T(1,128)S(1)} collective-permute-done((f32[1,128]{1,0:T(1,128)S(1)}, f32[1,128]{1,0:T(1,128)S(1)}, u32[]{:S(2)}, u32[]{:S(2)}) %collective-permute-start.5) | collective-permute-done | bytes 544 | tf_op jit(solution)/shard_map/ppermute | solution.py:98
  126.8 6.2 %collective-permute-done.6 = f32[1,128]{1,0:T(1,128)S(1)} collective-permute-done((f32[1,128]{1,0:T(1,128)S(1)}, f32[1,128]{1,0:T(1,128)S(1)}, u32[]{:S(2)}, u32[]{:S(2)}) %collective-permute-start.6) | collective-permute-done | bytes 544 | tf_op jit(solution)/shard_map/ppermute | solution.py:98
  133.0 6.2 %collective-permute-done.7 = f32[1,128]{1,0:T(1,128)S(1)} collective-permute-done((f32[1,128]{1,0:T(1,128)S(1)}, f32[1,128]{1,0:T(1,128)S(1)}, u32[]{:S(2)}, u32[]{:S(2)}) %collective-permute-start.7) | collective-permute-done | bytes 544 | tf_op jit(solution)/shard_map/ppermute | solution.py:98
  139.3 6.2 %collective-permute-done.8 = f32[1,128]{1,0:T(1,128)S(1)} collective-permute-done((f32[1,128]{1,0:T(1,128)S(1)}, f32[1,128]{1,0:T(1,128)S(1)}, u32[]{:S(2)}, u32[]{:S(2)}) %collective-permute-start.8) | collective-permute-done | bytes 544 | tf_op jit(solution)/shard_map/ppermute | solution.py:98
  145.6 17.1 %psum.7 = f32[8,128]{1,0:T(8,128)S(1)} all-reduce(f32[8,128]{1,0:T(8,128)S(1)} %fusion.16), channel_id=1, replica_groups=mesh['year'=8,'region'=4] {'year'}, use_global_device_ids=true, to_apply=%region_4.5 | all-reduce | flops 1024 | bytes 8192 | tf_op jit(solution)/shard_map/psum | solution.py:103
  162.7 0.5 multiply_subtract_fusion
  (30 shorter events, 1.1 us)
Async XLA Ops:
  7.2 92.2 %all-reduce.3.cloned.1.call-start = ((), (), s32[]{:S(2)}) async-start(), calls=%async_computation | async-start | bytes 2097152
  8.7 3.7 %collective-permute-start = (bf16[23,1]{1,0:T(8,128)(2,1)S(1)}, bf16[23,1]{1,0:T(8,128)(2,1)S(1)}, u32[]{:S(2)}, u32[]{:S(2)}) collective-permute-start(bf16[23,1]{1,0:T(8,128)(2,1)S(1)} %get-tuple-element.6), channel_id=1, source_target_pairs={{0,1},{1,2},{2,3},{3,0},{4,5},{5,6},{6,7},{7,4},{8,9},{9,10},{10,1... | collective-permute-start | bytes 146 | tf_op jit(solution)/shard_map/ppermute | solution.py:22
  9.2 3.4 %collective-permute-start.1 = (bf16[23,1]{1,0:T(8,128)(2,1)S(1)}, bf16[23,1]{1,0:T(8,128)(2,1)S(1)}, u32[]{:S(2)}, u32[]{:S(2)}) collective-permute-start(bf16[23,1]{1,0:T(8,128)(2,1)S(1)} %get-tuple-element.7), channel_id=1, source_target_pairs={{1,0},{2,1},{3,2},{0,3},{5,4},{6,5},{7,6},{4,7},{9,8},{10,9},{11,1... | collective-permute-start | bytes 146 | tf_op jit(solution)/shard_map/ppermute | solution.py:23
  16.9 1.9 %copy-start.1 = (u32[32]{0:T(128)S(1)}, u32[32]{0:T(128)}, u32[]{:S(2)}) copy-start(u32[32]{0:T(128)} %constant.93) | copy-start | bytes 388
  101.8 61.5 %copy-start = (f32[1,128]{1,0:T(1,128)}, f32[1,128]{1,0:T(1,128)S(1)}, u32[]{:S(2)}) copy-start(f32[1,128]{1,0:T(1,128)S(1)} %add_bitcast_fusion) | copy-start | bytes 1540
  101.8 6.3 %collective-permute-start.2 = (f32[1,128]{1,0:T(1,128)S(1)}, f32[1,128]{1,0:T(1,128)S(1)}, u32[]{:S(2)}, u32[]{:S(2)}) collective-permute-start(f32[1,128]{1,0:T(1,128)S(1)} %add_bitcast_fusion), channel_id=1, source_target_pairs={{0,4},{4,8},{8,12},{12,16},{16,20},{20,24},{24,28},{28,0},{1,5},{5... | collective-permute-start | bytes 1544 | tf_op jit(solution)/shard_map/ppermute | solution.py:98
  108.1 6.2 %collective-permute-start.3 = (f32[1,128]{1,0:T(1,128)S(1)}, f32[1,128]{1,0:T(1,128)S(1)}, u32[]{:S(2)}, u32[]{:S(2)}) collective-permute-start(f32[1,128]{1,0:T(1,128)S(1)} %collective-permute-done.2), channel_id=1, source_target_pairs={{0,4},{4,8},{8,12},{12,16},{16,20},{20,24},{24,28},{28,0},{1,5},{5... | collective-permute-start | bytes 1544 | tf_op jit(solution)/shard_map/ppermute | solution.py:98
  114.3 6.2 %collective-permute-start.4 = (f32[1,128]{1,0:T(1,128)S(1)}, f32[1,128]{1,0:T(1,128)S(1)}, u32[]{:S(2)}, u32[]{:S(2)}) collective-permute-start(f32[1,128]{1,0:T(1,128)S(1)} %collective-permute-done.3), channel_id=1, source_target_pairs={{0,4},{4,8},{8,12},{12,16},{16,20},{20,24},{24,28},{28,0},{1,5},{5... | collective-permute-start | bytes 1544 | tf_op jit(solution)/shard_map/ppermute | solution.py:98
  120.5 6.2 %collective-permute-start.5 = (f32[1,128]{1,0:T(1,128)S(1)}, f32[1,128]{1,0:T(1,128)S(1)}, u32[]{:S(2)}, u32[]{:S(2)}) collective-permute-start(f32[1,128]{1,0:T(1,128)S(1)} %collective-permute-done.4), channel_id=1, source_target_pairs={{0,4},{4,8},{8,12},{12,16},{16,20},{20,24},{24,28},{28,0},{1,5},{5... | collective-permute-start | bytes 1544 | tf_op jit(solution)/shard_map/ppermute | solution.py:98
  126.8 6.2 %collective-permute-start.6 = (f32[1,128]{1,0:T(1,128)S(1)}, f32[1,128]{1,0:T(1,128)S(1)}, u32[]{:S(2)}, u32[]{:S(2)}) collective-permute-start(f32[1,128]{1,0:T(1,128)S(1)} %collective-permute-done.5), channel_id=1, source_target_pairs={{0,4},{4,8},{8,12},{12,16},{16,20},{20,24},{24,28},{28,0},{1,5},{5... | collective-permute-start | bytes 1544 | tf_op jit(solution)/shard_map/ppermute | solution.py:98
  133.0 6.2 %collective-permute-start.7 = (f32[1,128]{1,0:T(1,128)S(1)}, f32[1,128]{1,0:T(1,128)S(1)}, u32[]{:S(2)}, u32[]{:S(2)}) collective-permute-start(f32[1,128]{1,0:T(1,128)S(1)} %collective-permute-done.6), channel_id=1, source_target_pairs={{0,4},{4,8},{8,12},{12,16},{16,20},{20,24},{24,28},{28,0},{1,5},{5... | collective-permute-start | bytes 1544 | tf_op jit(solution)/shard_map/ppermute | solution.py:98
  139.3 6.2 %collective-permute-start.8 = (f32[1,128]{1,0:T(1,128)S(1)}, f32[1,128]{1,0:T(1,128)S(1)}, u32[]{:S(2)}, u32[]{:S(2)}) collective-permute-start(f32[1,128]{1,0:T(1,128)S(1)} %collective-permute-done.7), channel_id=1, source_target_pairs={{0,4},{4,8},{8,12},{12,16},{16,20},{20,24},{24,28},{28,0},{1,5},{5... | collective-permute-start | bytes 1544 | tf_op jit(solution)/shard_map/ppermute | solution.py:98
Sparse Core Ops, SparseCore 0:
  18.9 80.3 all-reduce.2
